TPU v7x, 256 devices: a whole 4x4x8 slice. The times are simulated.
256 devices in a mesh: row: 32 (over z, x), col: 8 (over y, core).
Axes of the slice: x: 4, y: 4, z: 8, core: 2. Of those that a mesh axis runs over, the one named last changes fastest.
Arguments:
- tokens: bfloat16 [1024, 8192], P('row', 'col'), may hold values from -6 to 6
- cotangent: bfloat16 [1024, 8192], P('row', 'col'), may hold values from -6 to 6
- gate_weight: bfloat16 [8192, 16384], P('col', 'row'), may hold values from -0.125 to 0.125
- up_weight: bfloat16 [8192, 16384], P('col', 'row'), may hold values from -0.125 to 0.125
- down_weight: bfloat16 [16384, 8192], P('row', 'col'), may hold values from -0.078125 to 0.078125
- gate_mask: int32 [64, 128], P('col', 'row'), may hold values 0 or 1
- up_mask: int32 [64, 128], P('col', 'row'), may hold values 0 or 1
- down_mask: int32 [128, 64], P('row', 'col'), may hold values 0 or 1
Outputs:
- layer_out: bfloat16 [1024, 8192], P('row', 'col')
- grad_tokens: bfloat16 [1024, 8192], P('row', 'col')
- grad_gate_weight: float32 [8192, 16384], P('col', 'row')
- grad_up_weight: float32 [8192, 16384], P('col', 'row')
- grad_down_weight: float32 [16384, 8192], P('row', 'col')
All inputs are finite; a program needn't handle non-finite values. No bound on the sum of `gate_mask` or of `up_mask` or of `down_mask` on one device may be relied on, other than what follows from the above.
Results may differ from a plain program's by a relative error of at most 0.0049.
Values may be sent and summed in bfloat16 or wider, within the bound.
No kernel may reach another device: no remote copies, remote signals or barrier semaphores. Data moves between devices by JAX's collectives and lax.ppermute only.
A program may use at most 128 MiB of HBM per device.

v0:
```python
import jax
import jax.numpy as jnp
from jax import lax
from jax.sharding import PartitionSpec as P

BLOCK = 128
contract_inner = (((1,), (1,)), ((), ()))
contract_outer = (((0,), (0,)), ((), ()))


def apply_pattern(weight, pattern):
    row_blocks, col_blocks = pattern.shape
    block_scale = pattern.astype(weight.dtype)
    blocks = weight.reshape(row_blocks, BLOCK, col_blocks, BLOCK) * block_scale[:, None, :, None]
    return blocks.reshape(weight.shape)


def col_reduce(summands, finish):
    summed = lax.psum(summands, "col")
    return finish(summed)


def shards(tokens, cotangent, gate_weight, up_weight, down_weight, gate_mask, up_mask, down_mask):
    hidden_width = gate_weight.shape[1]
    gathered_tokens, gathered_grads = (
        lax.all_gather(tokens, "row", axis=0, tiled=True),
        lax.all_gather(cotangent, "row", axis=0, tiled=True),
    )
    joint_weight = jnp.concatenate(
        [apply_pattern(gate_weight, gate_mask), apply_pattern(up_weight, up_mask)], axis=1
    )
    masked_down = apply_pattern(down_weight, down_mask)
    joint_part = jnp.dot(gathered_tokens, joint_weight, preferred_element_type=jnp.float32)

    def activate(joint_pre):
        gate_pre = joint_pre[:, :hidden_width]
        up_pre = joint_pre[:, hidden_width:]
        hidden_rows = (gate_pre * jax.nn.sigmoid(gate_pre) * up_pre).astype(jnp.bfloat16)
        return (hidden_rows, joint_pre)

    hidden, joint_pre = col_reduce(joint_part, activate)
    hidden_part = lax.dot_general(
        gathered_grads, masked_down, contract_inner, preferred_element_type=jnp.float32
    )

    def derive(grad_hidden):
        gate_pre = joint_pre[:, :hidden_width]
        up_pre = joint_pre[:, hidden_width:]
        sigmoid_gate = jax.nn.sigmoid(gate_pre)
        silu_gate = gate_pre * sigmoid_gate
        grad_gate_pre = (
            grad_hidden * up_pre * sigmoid_gate * (1.0 + gate_pre * (1.0 - sigmoid_gate))
        )
        grad_up_pre = grad_hidden * silu_gate
        joint_rows = jnp.concatenate(
            [grad_gate_pre.astype(jnp.bfloat16), grad_up_pre.astype(jnp.bfloat16)], axis=1
        )
        return (joint_rows, grad_hidden)

    joint_grad, unused = col_reduce(hidden_part, derive)
    output_term = jnp.dot(hidden, masked_down, preferred_element_type=jnp.float32)
    token_term = lax.dot_general(
        joint_grad, joint_weight, contract_inner, preferred_element_type=jnp.float32
    )
    layer_out, grad_tokens = (
        lax.psum_scatter(output_term, "row", scatter_dimension=0, tiled=True),
        lax.psum_scatter(token_term, "row", scatter_dimension=0, tiled=True),
    )
    weight_grads = lax.dot_general(
        gathered_tokens, joint_grad, contract_outer, preferred_element_type=jnp.float32
    )
    grad_gate_weight = apply_pattern(weight_grads[:, :hidden_width], gate_mask)
    grad_up_weight = apply_pattern(weight_grads[:, hidden_width:], up_mask)
    grad_down_weight = apply_pattern(
        lax.dot_general(hidden, gathered_grads, contract_outer, preferred_element_type=jnp.float32),
        down_mask,
    )
    return (
        layer_out.astype(jnp.bfloat16),
        grad_tokens.astype(jnp.bfloat16),
        grad_gate_weight,
        grad_up_weight,
        grad_down_weight,
    )


def solution(mesh):
    in_specs = (
        P("row", "col"),
        P("row", "col"),
        P("col", "row"),
        P("col", "row"),
        P("row", "col"),
        P("col", "row"),
        P("col", "row"),
        P("row", "col"),
    )
    out_specs = (
        P("row", "col"),
        P("row", "col"),
        P("col", "row"),
        P("col", "row"),
        P("row", "col"),
    )
    return jax.shard_map(shards, mesh=mesh, in_specs=in_specs, out_specs=out_specs, check_vma=False)
```

profile of v0, /device:TPU:8, one launch (start us, length us, event | category | flops | bytes accessed | tf_op | source)
XLA Modules:
  0.0 727.5 jit_solution(3877633077299212398)
XLA Ops:
  7.2 0.0 copy-start.6
  7.2 0.0 copy-start.5
  7.2 0.0 all-gather.3.cloned.1.call-start
  7.2 0.7 all-gather.3.cloned.1.call-update
  7.9 0.0 all-gather.5.cloned.1.call-start
  8.0 0.7 all-gather.5.cloned.1.call-update
  8.7 0.0 all-reduce.3.cloned.1.call-start
  8.7 0.8 fusion.8
  9.5 0.1 copy.13
  9.6 0.8 fusion.7
  10.3 0.1 copy.14
  10.4 0.8 fusion.6
  11.2 0.3 mul.88
  11.5 0.3 mul.91
  11.9 0.0 copy-done.6
  11.9 0.0 copy-done.5
  11.9 1.3 bitcast_multiply_fusion.4
  13.2 0.0 copy-start.7
  13.2 78.2 %all-gather.3.cloned.1.call-done = bf16[1024,1024]{1,0:T(8,128)(2,1)} async-done(((bf16[32,1024]{1,0:T(8,128)(2,1)}), bf16[1024,1024]{1,0:T(8,128)(2,1)}) %all-gather.3.cloned.1.call-update) | async-done | bytes 2097168 | tf_op jit(solution)/shard_map/all_gather | solution.py:26
  91.4 0.0 copy-start
  91.4 6.4 convolution_bitcast_fusion.1
  97.8 0.0 copy-done.7
  97.8 71.4 %all-gather.5.cloned.1.call-done = bf16[1024,1024]{1,0:T(8,128)(2,1)} async-done(((bf16[32,1024]{1,0:T(8,128)(2,1)}), bf16[1024,1024]{1,0:T(8,128)(2,1)}) %all-gather.5.cloned.1.call-update) | async-done | bytes 2097168 | tf_op jit(solution)/shard_map/all_gather | solution.py:27
  169.2 0.2 mul.96
  169.4 0.0 copy-done
  169.4 4.2 convolution_bitcast_fusion.2
  173.6 0.0 all-reduce.3.cloned.1.call-update
  173.6 0.0 reduce-scatter.5.cloned.1.call-start
  173.7 84.3 %all-reduce.3.cloned.1.call-done = (f32[1024,1024]{0,1:T(8,128)}, f32[1024,512]{0,1:T(8,128)}) async-done(((f32[1024,1024]{0,1:T(8,128)}, f32[1024,512]{0,1:T(8,128)}), (f32[1024,1024]{0,1:T(8,128)}, f32[1024,512]{0,1:T(8,128)})) %all-reduce.3.cloned.1.call-update) | async-done | bytes 6291472 | tf_op jit(solution)/shard_map/psum | solution.py:19
  258.0 0.0 copy-start.8
  258.0 0.0 copy-start.9
  258.0 4.4 multiply_convert_fusion.1
  262.3 0.0 copy-start.1
  262.4 0.0 copy-start.3
  262.4 1.0 copy-done.1
  263.4 0.3 copy-done.3
  263.7 0.0 copy-done.8
  263.7 0.0 copy-done.9
  263.7 4.4 fusion.1
  268.1 0.0 reduce-scatter.5.cloned.1.call-update
  268.1 0.2 reduce-scatter.3.cloned.1.call-start
  268.3 3.3 fusion.2
  271.6 0.0 copy-start.2
  271.6 0.0 copy-start.4
  271.6 0.0 reduce-scatter.3.cloned.1.call-update
  271.6 1.2 copy-done.2
  272.8 0.3 copy-done.4
  273.1 3.9 convolution_bitcast_fusion
  277.0 0.2 mul.104
  277.2 0.2 mul.107
  277.4 2.8 bitcast_multiply_fusion.1
  280.3 2.9 copy.15
  283.2 1.8 copy.16
  285.0 0.0 copy-start.10
  285.0 0.2 mul.110
  285.2 1.4 copy-done.10
  286.6 2.7 bitcast_multiply_fusion
  289.3 204.7 %reduce-scatter.5.cloned.1.call-done = f32[32,1024]{1,0:T(8,128)} async-done(((f32[1024,1024]{1,0:T(8,128)}), f32[32,1024]{1,0:T(8,128)}) %reduce-scatter.5.cloned.1.call-update) | async-done | bytes 131088 | tf_op jit(solution)/shard_map/reduce_scatter | solution.py:67
  494.0 1.5 convert_element_type.40
  495.5 223.9 %reduce-scatter.3.cloned.1.call-done = f32[32,1024]{1,0:T(8,128)} async-done(((f32[1024,1024]{1,0:T(8,128)}), f32[32,1024]{1,0:T(8,128)}) %reduce-scatter.3.cloned.1.call-update) | async-done | bytes 131088 | tf_op jit(solution)/shard_map/reduce_scatter | solution.py:66
  719.5 1.5 convert_element_type.37
Async XLA Ops:
  7.2 4.7 copy-start.6
  7.2 4.7 copy-start.5
  7.2 84.2 %all-gather.3.cloned.1.call-start = ((), (), s32[]{:S(2)}) async-start(), calls=%async_computation.2 | async-start | bytes 2162688 | tf_op jit(solution)/shard_map/all_gather | solution.py:26
  7.9 161.2 %all-gather.5.cloned.1.call-start = ((), (), s32[]{:S(2)}) async-start(), calls=%async_computation.4 | async-start | bytes 2162688 | tf_op jit(solution)/shard_map/all_gather | solution.py:27
  8.7 249.3 %all-reduce.3.cloned.1.call-start = ((), (), s32[]{:S(2)}) async-start(), calls=%async_computation.6 | async-start | bytes 12582912 | tf_op jit(solution)/shard_map/psum | solution.py:19
  13.2 84.6 %copy-start.7 = (bf16[1024,512]{1,0:T(8,128)(2,1)}, bf16[1024,512]{1,0:T(8,128)(2,1)S(1)}, u32[]{:S(2)}) copy-start(bf16[1024,512]{1,0:T(8,128)(2,1)S(1)} %get-tuple-element.23) | copy-start | bytes 3145732
  91.4 78.0 %copy-start = (bf16[512,1024]{1,0:T(8,128)(2,1)S(1)}, bf16[512,1024]{1,0:T(8,128)(2,1)}, u32[]{:S(2)}) copy-start(bf16[512,1024]{1,0:T(8,128)(2,1)} %param.12) | copy-start | bytes 3145732
  173.6 320.4 %reduce-scatter.5.cloned.1.call-start = ((), (), s32[]{:S(2)}) async-start(), calls=%async_computation.5 | async-start | bytes 4325376 | tf_op jit(solution)/shard_map/reduce_scatter | solution.py:67
  258.0 5.7 copy-start.8
  258.0 5.7 copy-start.9
  262.3 1.0 copy-start.1
  262.4 1.3 copy-start.3
  268.1 451.4 %reduce-scatter.3.cloned.1.call-start = ((), (), s32[]{:S(2)}) async-start(), calls=%async_computation.3 | async-start | bytes 4325376 | tf_op jit(solution)/shard_map/reduce_scatter | solution.py:66
  271.6 1.2 copy-start.2
  271.6 1.5 copy-start.4
  285.0 1.6 copy-start.10
Sparse Core Ops, SparseCore 0:
  10.6 80.7 all-gather.2
  94.0 75.1 all-gather.4
  173.7 84.1 all-reduce.2
  268.2 225.7 reduce-scatter.4
  497.7 221.6 reduce-scatter.2
where the time goes:
time: 728 us
  waiting for transfers between devices  664 us (91%)
  matrix products  24.9 us (3%)
  other arithmetic  13.9 us (2%)
  between operations  13.9 us (2%)
  local copies, waits for them, and re-layouts  10.6 us (1%)
    reduce_scatter x1, waiting for transfers between devices, shards(): lax.psum_scatter(output_term, 'row', scatter_dimension=0, tiled=True)  224 us
    reduce_scatter x1, waiting for transfers between devices, shards(): lax.psum_scatter(token_term, 'row', scatter_dimension=0, tiled=True)  205 us
    psum x1, waiting for transfers between devices, col_reduce(): summed = lax.psum(summands, 'col')  84.3 us
    all_gather x1, waiting for transfers between devices, shards(): lax.all_gather(tokens, 'row', axis=0, tiled=True)  78.2 us
    all_gather x1, waiting for transfers between devices, shards(): lax.all_gather(cotangent, 'row', axis=0, tiled=True)  71.4 us
  transfers between devices with their start and end apart: 5, of which 5 were waited for; matrix products, arithmetic and copies ran while one was open for 4% of the time, Pallas kernels for 0%

commit v1 on v0

--- a/solution.py
+++ b/solution.py
@@ -16,7 +16,9 @@
 
 
 def col_reduce(summands, finish):
-    summed = lax.psum(summands, "col")
+    summed = summands
+    for hop in (1, 2, 4):
+        summed = summed + lax.ppermute(summed, "col", [(dev, dev ^ hop) for dev in range(8)])
     return finish(summed)
 
 

time: 728 us -> 856 us (1.18)
  waiting for transfers between devices: 664 us -> 776 us
  other arithmetic: 13.9 us -> 25.4 us
    ppermute x0 -> x6, waiting for transfers between devices: none -> 216 us  [col_reduce(): lax.ppermute(summed, 'col', [(dev, dev ^ hop) for dev in range(8)])]
    psum x1 -> x0, waiting for transfers between devices: 84.3 us -> none  [col_reduce(): summed = lax.psum(summands, 'col')]
    reduce_scatter x1, waiting for transfers between devices: 224 us -> 195 us  [shards(): lax.psum_scatter(output_term, 'row', scatter_dimension=0, tiled=True)]
    reduce_scatter x1, waiting for transfers between devices: 205 us -> 224 us  [shards(): lax.psum_scatter(token_term, 'row', scatter_dimension=0, tiled=True)]
    add x0 -> x5, other arithmetic: none -> 13.6 us  [col_reduce(): summed + lax.ppermute(summed, 'col', [(dev, dev ^ hop) for dev in range(8)])]
    all_gather x1, waiting for transfers between devices: 71.4 us -> 60.5 us  [shards(): lax.all_gather(cotangent, 'row', axis=0, tiled=True)]
  transfers between devices with their start and end apart: 5 -> 10, of which waited for: 5 -> 9; matrix products, arithmetic and copies ran while one was open for 4% -> 4% of each run, Pallas kernels for 0% -> 0%
where the time goes in v1:
time: 856 us; the launch traced here: 855 us
  waiting for transfers between devices  776 us (91%)
  other arithmetic  25.4 us (3%)
  matrix products  25 us (3%)
  between operations  13.9 us (2%)
  local copies, waits for them, and re-layouts  10.8 us (1%)
    reduce_scatter x1, waiting for transfers between devices, shards(): lax.psum_scatter(token_term, 'row', scatter_dimension=0, tiled=True)  224 us
    ppermute x6, waiting for transfers between devices, col_reduce(): lax.ppermute(summed, 'col', [(dev, dev ^ hop) for dev in range(8)])  216 us
    reduce_scatter x1, waiting for transfers between devices, shards(): lax.psum_scatter(output_term, 'row', scatter_dimension=0, tiled=True)  195 us
    all_gather x1, waiting for transfers between devices, shards(): lax.all_gather(tokens, 'row', axis=0, tiled=True)  79.7 us
    all_gather x1, waiting for transfers between devices, shards(): lax.all_gather(cotangent, 'row', axis=0, tiled=True)  60.5 us
  transfers between devices with their start and end apart: 10, of which 9 were waited for; matrix products, arithmetic and copies ran while one was open for 4% of the time, Pallas kernels for 0%

profile of v1, /device:TPU:8, one launch (start us, length us, event | category | flops | bytes accessed | tf_op | source)
XLA Modules:
  0.0 855.5 jit_solution(18088486989898646379)
XLA Ops:
  7.2 0.0 copy-start.1
  7.2 0.0 copy-start.2
  7.2 0.0 all-gather.3.cloned.1.call-start
  7.2 0.7 all-gather.3.cloned.1.call-update
  7.9 0.0 all-gather.5.cloned.1.call-start
  8.0 0.8 fusion.7
  8.7 0.1 copy.14
  8.8 0.8 fusion.8
  9.6 0.1 copy.13
  9.7 0.3 mul.91
  10.0 0.3 mul.88
  10.4 0.0 copy-done.1
  10.4 0.0 copy-done.2
  10.4 1.3 bitcast_multiply_fusion.4
  11.7 79.7 %all-gather.3.cloned.1.call-done = bf16[1024,1024]{1,0:T(8,128)(2,1)} async-done(((bf16[32,1024]{1,0:T(8,128)(2,1)}), bf16[1024,1024]{1,0:T(8,128)(2,1)}) %all-gather.3.cloned.1.call-update) | async-done | bytes 2097168 | tf_op jit(solution)/shard_map/all_gather | solution.py:28
  91.4 6.3 convolution_bitcast_fusion.1
  97.7 0.0 copy-done.3
  97.7 0.0 collective-permute-start
  97.7 0.0 all-gather.5.cloned.1.call-update
  97.8 0.0 copy-start.8
  97.8 0.0 copy-start
  97.8 0.0 reduce-scatter.3.cloned.1.call-start
  97.8 7.4 collective-permute-done
  105.2 6.9 add.29
  112.2 0.5 collective-permute-start.1
  112.7 60.5 %all-gather.5.cloned.1.call-done = bf16[1024,1024]{1,0:T(8,128)(2,1)} async-done(((bf16[32,1024]{1,0:T(8,128)(2,1)}), bf16[1024,1024]{1,0:T(8,128)(2,1)}) %all-gather.5.cloned.1.call-update) | async-done | bytes 2097168 | tf_op jit(solution)/shard_map/all_gather | solution.py:29
  173.2 0.2 mul.96
  173.4 2.9 convolution_bitcast_fusion.2
  176.3 0.1 collective-permute-start.3
  176.4 4.1 collective-permute-done.3
  180.6 0.6 add.33
  181.1 24.0 %collective-permute-done.1 = f32[1024,1024]{0,1:T(8,128)} collective-permute-done((f32[1024,1024]{0,1:T(8,128)}, f32[1024,1024]{0,1:T(8,128)}, u32[]{:S(2)}, u32[]{:S(2)}) %collective-permute-start.1) | collective-permute-done | bytes 4194336 | tf_op jit(solution)/shard_map/ppermute | solution.py:21
  205.1 4.4 add.30
  209.5 2.2 collective-permute-start.2
  211.7 1.4 collective-permute-start.4
  213.1 134.7 %collective-permute-done.4 = f32[1024,512]{0,1:T(8,128)S(1)} collective-permute-done((f32[1024,512]{0,1:T(8,128)S(1)}, f32[1024,512]{0,1:T(8,128)S(1)}, u32[]{:S(2)}, u32[]{:S(2)}) %collective-permute-start.4) | collective-permute-done | bytes 2097184 | tf_op jit(solution)/shard_map/ppermute | solution.py:21
  347.8 0.4 add.34
  348.2 0.3 collective-permute-start.5
  348.5 0.0 collective-permute-done.2
  348.5 1.4 add.31
  349.8 46.1 %collective-permute-done.5 = f32[1024,512]{0,1:T(8,128)S(1)} collective-permute-done((f32[1024,512]{0,1:T(8,128)S(1)}, f32[1024,512]{0,1:T(8,128)S(1)}, u32[]{:S(2)}, u32[]{:S(2)}) %collective-permute-start.5) | collective-permute-done | bytes 2097184 | tf_op jit(solution)/shard_map/ppermute | solution.py:21
  395.9 3.1 multiply_convert_fusion.1
  399.0 3.3 fusion.2
  402.2 0.0 reduce-scatter.3.cloned.1.call-update
  402.3 0.0 reduce-scatter.5.cloned.1.call-start
  402.3 1.1 copy-done.4
  403.5 0.3 copy-done.5
  403.8 6.0 fusion.1
  409.7 0.0 reduce-scatter.5.cloned.1.call-update
  409.8 1.3 copy-done.6
  411.0 0.3 copy-done.7
  411.4 3.9 convolution_bitcast_fusion
  415.3 0.2 mul.107
  415.5 0.2 mul.104
  415.7 2.8 bitcast_multiply_fusion.1
  418.5 2.9 copy.15
  421.4 1.8 copy.16
  423.2 0.2 mul.110
  423.4 1.4 copy-done.9
  424.8 2.7 bitcast_multiply_fusion
  427.5 194.6 %reduce-scatter.3.cloned.1.call-done = f32[32,1024]{1,0:T(8,128)} async-done(((f32[1024,1024]{1,0:T(8,128)}), f32[32,1024]{1,0:T(8,128)}) %reduce-scatter.3.cloned.1.call-update) | async-done | bytes 131088 | tf_op jit(solution)/shard_map/reduce_scatter | solution.py:68
  622.2 1.5 convert_element_type.37
  623.7 223.7 %reduce-scatter.5.cloned.1.call-done = f32[32,1024]{1,0:T(8,128)} async-done(((f32[1024,1024]{1,0:T(8,128)}), f32[32,1024]{1,0:T(8,128)}) %reduce-scatter.5.cloned.1.call-update) | async-done | bytes 131088 | tf_op jit(solution)/shard_map/reduce_scatter | solution.py:69
  847.4 1.5 convert_element_type.40
  (9 shorter events, 0.0 us)
Async XLA Ops:
  7.2 3.2 copy-start.1
  7.2 3.2 copy-start.2
  7.2 84.2 %all-gather.3.cloned.1.call-start = ((), (), s32[]{:S(2)}) async-start(), calls=%async_computation.2 | async-start | bytes 2162688 | tf_op jit(solution)/shard_map/all_gather | solution.py:28
  7.9 165.3 %all-gather.5.cloned.1.call-start = ((), (), s32[]{:S(2)}) async-start(), calls=%async_computation.4 | async-start | bytes 2162688 | tf_op jit(solution)/shard_map/all_gather | solution.py:29
  11.7 86.0 %copy-start.3 = (bf16[1024,512]{1,0:T(8,128)(2,1)}, bf16[1024,512]{1,0:T(8,128)(2,1)S(1)}, u32[]{:S(2)}) copy-start(bf16[1024,512]{1,0:T(8,128)(2,1)S(1)} %get-tuple-element.21) | copy-start | bytes 3145732
  97.7 7.5 collective-permute-start
  97.8 14.9 %copy-start.8 = (s32[4,8]{1,0:T(4,128)S(1)}, s32[4,8]{1,0:T(4,128)}, u32[]{:S(2)}) copy-start(s32[4,8]{1,0:T(4,128)} %param.15) | copy-start | bytes 388
  97.8 75.7 %copy-start = (bf16[512,1024]{1,0:T(8,128)(2,1)S(1)}, bf16[512,1024]{1,0:T(8,128)(2,1)}, u32[]{:S(2)}) copy-start(bf16[512,1024]{1,0:T(8,128)(2,1)} %param.12) | copy-start | bytes 3145732
  97.8 524.4 %reduce-scatter.3.cloned.1.call-start = ((), (), s32[]{:S(2)}) async-start(), calls=%async_computation.3 | async-start | bytes 4325376 | tf_op jit(solution)/shard_map/reduce_scatter | solution.py:68
  112.2 92.9 %collective-permute-start.1 = (f32[1024,1024]{0,1:T(8,128)}, f32[1024,1024]{0,1:T(8,128)}, u32[]{:S(2)}, u32[]{:S(2)}) collective-permute-start(f32[1024,1024]{0,1:T(8,128)} %add.29), channel_id=1, source_target_pairs={{0,2},{1,3},{2,0},{3,1},{4,6},{5,7},{6,4},{7,5},{8,10},{9,11},{10,... | collective-permute-start | bytes 12582920 | tf_op jit(solution)/shard_map/ppermute | solution.py:21
  176.3 4.2 collective-permute-start.3
  209.5 139.0 %collective-permute-start.2 = (f32[1024,1024]{0,1:T(8,128)S(1)}, f32[1024,1024]{0,1:T(8,128)S(1)}, u32[]{:S(2)}, u32[]{:S(2)}) collective-permute-start(f32[1024,1024]{0,1:T(8,128)S(1)} %add.30), channel_id=1, source_target_pairs={{0,4},{1,5},{2,6},{3,7},{4,0},{5,1},{6,2},{7,3},{8,12},{9,13},{10,... | collective-permute-start | bytes 12582920 | tf_op jit(solution)/shard_map/ppermute | solution.py:21
  211.7 136.1 %collective-permute-start.4 = (f32[1024,512]{0,1:T(8,128)S(1)}, f32[1024,512]{0,1:T(8,128)S(1)}, u32[]{:S(2)}, u32[]{:S(2)}) collective-permute-start(f32[1024,512]{0,1:T(8,128)S(1)} %add.33), channel_id=1, source_target_pairs={{0,2},{1,3},{2,0},{3,1},{4,6},{5,7},{6,4},{7,5},{8,10},{9,11},{10,... | collective-permute-start | bytes 6291464 | tf_op jit(solution)/shard_map/ppermute | solution.py:21
  348.2 47.7 %collective-permute-start.5 = (f32[1024,512]{0,1:T(8,128)S(1)}, f32[1024,512]{0,1:T(8,128)S(1)}, u32[]{:S(2)}, u32[]{:S(2)}) collective-permute-start(f32[1024,512]{0,1:T(8,128)S(1)} %add.34), channel_id=1, source_target_pairs={{0,4},{1,5},{2,6},{3,7},{4,0},{5,1},{6,2},{7,3},{8,12},{9,13},{10,... | collective-permute-start | bytes 6291464 | tf_op jit(solution)/shard_map/ppermute | solution.py:21
  402.2 1.2 copy-start.4
  402.2 1.5 copy-start.5
  402.3 445.1 %reduce-scatter.5.cloned.1.call-start = ((), (), s32[]{:S(2)}) async-start(), calls=%async_computation.5 | async-start | bytes 4325376 | tf_op jit(solution)/shard_map/reduce_scatter | solution.py:69
  409.7 1.3 copy-start.6
  409.7 1.6 copy-start.7
  423.2 1.6 copy-start.9
Sparse Core Ops, SparseCore 0:
  10.6 80.7 all-gather.2
  97.9 75.2 all-gather.4
  402.4 219.7 reduce-scatter.2
  625.9 221.4 reduce-scatter.4
